TPU v7x, 32 devices: a whole 2x2x4 slice. The times are simulated.
32 devices in a mesh: groups: 2 (over y), seq: 4 (over z), head: 2 (over x), sub: 2 (over core).
Axes of the slice: x: 2, y: 2, z: 4, core: 2. Of those that a mesh axis runs over, the one named last changes fastest.
Arguments:
- queries: bfloat16 [64, 1024, 128], P(('head', 'sub'), ('groups', 'seq')), parts along dimension 1, may hold values from -6 to 6
- keys_values: bfloat16 [8, 1024, 256], P(('head', 'sub'), ('groups', 'seq')), parts along dimension 1, may hold values from -6 to 6
- student_x: bfloat16 [64, 1024, 128], P(('head', 'sub'), ('groups', 'seq')), parts along dimension 1, may hold values from -32 to 32
- state_maps: bfloat16 [8, 1024, 128], P(('head', 'sub'), ('groups', 'seq')), parts along dimension 1, may hold values from -0.75 to 0.75
- decay_logit: float32 [64, 1024], P(('head', 'sub'), ('groups', 'seq')), parts along dimension 1, may hold values from 0 to 16
- skip_gain: float32 [64], P(('head', 'sub')), may hold values from 0.5 to 2
- init_state: float32 [128, 64, 128], P(('groups', 'head', 'sub')), parts along dimension 0, may hold values from -6 to 6
Outputs:
- grad_x: bfloat16 [64, 1024, 128], P(('head', 'sub'), ('groups', 'seq')), parts along dimension 1
- grad_maps: bfloat16 [8, 1024, 128], P(('head', 'sub'), ('groups', 'seq')), parts along dimension 1
- grad_log_decay: float32 [64, 1024], P(('head', 'sub'), ('groups', 'seq')), parts along dimension 1
There are 2 independent parts, one for each index of `groups`. A program takes and returns all parts, laid end to end along the dimension named above; an argument that names none is the same for every part. Nothing has to cross between parts.
All inputs are finite; a program needn't handle non-finite values.
Results may differ from a plain program's by a relative error of at most 0.013.
Values may be sent and summed in bfloat16 or wider, within the bound.
No kernel may reach another device: no remote copies, remote signals or barrier semaphores. Data moves between devices by JAX's collectives and lax.ppermute only.
A program may use at most 64 MiB of HBM per device.

v0:
```python
import math
import jax
import jax.numpy as jnp
from jax import lax
from jax.sharding import PartitionSpec as P

epsilon = 1e-05
highest = lax.Precision.HIGHEST


def entering_2(x, axis, join, neutral):
    place = lax.axis_index(axis)
    gathered = jax.tree.map(
        lambda a, kind: lax.all_gather(a.astype(kind), axis), x, (jnp.bfloat16, jnp.bfloat16)
    )
    state = jax.tree.map(lambda a, e: jnp.zeros_like(a) + jnp.asarray(e, a.dtype), x, neutral)

    def entering_one(turn, state):
        return join(
            state,
            jax.tree.map(
                lambda a, own: lax.dynamic_index_in_dim(a, turn, 0, False).astype(own.dtype),
                gathered,
                x,
            ),
        )

    return lax.fori_loop(0, place, entering_one, state)


def prefix(x, axis, join, neutral):
    count = lax.axis_size(axis)
    place = lax.axis_index(axis)
    ahead = count - 1 - place
    gathered = jax.tree.map(
        lambda a, kind: lax.all_gather(a.astype(kind), axis),
        x,
        jax.tree.map(lambda a: jnp.bfloat16 if a.dtype == jnp.float32 else a.dtype, x),
    )
    state = jax.tree.map(lambda a, e: jnp.zeros_like(a) + jnp.asarray(e, a.dtype), x, neutral)

    def prefix_one(turn, state):
        source = count - 1 - turn
        return join(
            state,
            jax.tree.map(
                lambda a, own: lax.dynamic_index_in_dim(a, source, 0, False).astype(own.dtype),
                gathered,
                x,
            ),
        )

    return lax.fori_loop(0, ahead, prefix_one, state)


def attend(query_rows, positions, keys_values, tok_dev):
    group_count, row_count, head_width = query_rows.shape
    score_scale = head_width ** (-0.5)
    start_max = jnp.full((group_count, row_count), -1e30, jnp.float32)
    start_sum = jnp.zeros((group_count, row_count), jnp.float32)
    start_acc = jnp.zeros((group_count, row_count, head_width), jnp.float32)
    shards = lax.all_gather(keys_values, "seq", axis=1, tiled=True)
    block_rows = math.gcd(shards.shape[1], tok_dev)

    def one_block(number, running):
        running_max, running_sum, weighted = running
        key_block = lax.dynamic_slice_in_dim(shards, number * block_rows, block_rows, 1)
        scores = (
            jnp.einsum(
                "grd,gkd->grk",
                query_rows,
                key_block[:, :, :head_width],
                preferred_element_type=jnp.float32,
            )
            * score_scale
        )
        key_positions = number * block_rows + jnp.arange(block_rows)
        allowed = (positions[:, None] >= key_positions[None, :])[None]
        scores = jnp.where(allowed, scores, -1e30)
        new_max = jnp.maximum(running_max, jnp.max(scores, axis=2))
        weights = jnp.where(allowed, jnp.exp(scores - new_max[..., None]), 0.0)
        factor = jnp.exp(running_max - new_max)
        running_sum = running_sum * factor + jnp.sum(weights, axis=2)
        weighted = weighted * factor[..., None] + jnp.einsum(
            "grk,gkd->grd",
            weights.astype(jnp.bfloat16),
            key_block[:, :, head_width:],
            preferred_element_type=jnp.float32,
        )
        return (new_max, running_sum, weighted)

    running_max, running_sum, weighted = lax.fori_loop(
        0, shards.shape[1] // block_rows, one_block, (start_max, start_sum, start_acc)
    )
    return (weighted / running_sum[..., None]).astype(jnp.bfloat16)


def forward_chain(earlier, later):
    return (earlier[0] * later[0], later[0][:, None, None] * earlier[1] + later[1])


def backward_chain(earlier, later):
    decay_early, state_early, closing_early, sums_early = earlier
    decay_late, state_late, closing_late, sums_late = later
    return (
        decay_early * decay_late,
        decay_late[:, None, None] * state_early + state_late,
        closing_early + decay_early[:, None, None] * closing_late,
        sums_early + sums_late - jnp.sum(closing_late * state_early, axis=(1, 2)),
    )


def body(queries, keys_values, student_x, state_maps, decay_logit, skip_gain, init_state):
    local_heads, tok_dev, head_width = student_x.shape
    local_groups = state_maps.shape[0]
    per_group = local_heads // local_groups
    state_size = state_maps.shape[2] // 2
    seq_count = lax.axis_size("seq")
    seq_rank = lax.axis_index("seq")
    repeat_count = max(1, seq_count // per_group)
    sub_rows = tok_dev // repeat_count
    per_peer = per_group * repeat_count // seq_count
    sectioned = queries.reshape(local_groups, per_group * repeat_count, sub_rows, head_width)
    arrived = lax.all_to_all(sectioned, "seq", split_axis=1, concat_axis=1, tiled=True)
    slot_ids = jnp.arange(seq_count * per_peer)
    source = slot_ids // per_peer
    member = seq_rank * per_peer + slot_ids % per_peer
    starts = source * tok_dev + member % repeat_count * sub_rows
    positions = (starts[:, None] + jnp.arange(sub_rows)[None, :]).reshape(-1)
    answers = attend(arrived.reshape(local_groups, -1, head_width), positions, keys_values, tok_dev)
    answers = answers.reshape(local_groups, seq_count * per_peer, sub_rows, head_width)
    teacher = lax.all_to_all(answers, "seq", split_axis=1, concat_axis=1, tiled=True).reshape(
        local_heads, tok_dev, head_width
    )
    teacher_wide = teacher.astype(jnp.float32)
    target = teacher_wide * lax.rsqrt(
        jnp.mean(teacher_wide * teacher_wide, axis=2, keepdims=True) + epsilon
    )
    log_decay = jax.nn.log_sigmoid(decay_logit)
    cumulative = jnp.cumsum(log_decay, axis=1)
    totals = cumulative[:, -1]
    decays = jnp.exp(totals)
    to_end = jnp.exp(totals[:, None] - cumulative)
    from_start = jnp.exp(cumulative)
    in_maps = state_maps[:, :, :state_size]
    out_maps = state_maps[:, :, state_size:]
    intersection = jnp.einsum("gtn,gsn->gts", out_maps, in_maps, preferred_element_type=jnp.float32)
    order_ids = jnp.arange(tok_dev)
    causal = (order_ids[:, None] >= order_ids[None, :])[None]
    gaps = cumulative[:, :, None] - cumulative[:, None, :]
    decayed = jnp.where(causal, jnp.exp(jnp.where(causal, gaps, 0.0)), 0.0)
    mixing = (
        decayed.reshape(local_groups, per_group, tok_dev, tok_dev) * intersection[:, None]
    ).reshape(local_heads, tok_dev, tok_dev)
    inputs_wide = student_x.astype(jnp.float32)
    in_heads = jnp.repeat(in_maps.astype(jnp.float32), per_group, axis=0)
    out_heads = jnp.repeat(out_maps.astype(jnp.float32), per_group, axis=0)
    local_out = jnp.einsum("hts,hsp->htp", mixing, inputs_wide, precision=highest)
    weighted_in = in_heads * to_end[..., None]
    end_state = jnp.einsum("hsn,hsp->hnp", weighted_in, inputs_wide, precision=highest)
    prefix_decay, prefix_state = entering_2(
        (decays, end_state),
        "seq",
        forward_chain,
        (jnp.ones_like(decays), jnp.zeros_like(end_state)),
    )
    entering = prefix_state + prefix_decay[:, None, None] * init_state
    state_out = local_out + from_start[..., None] * jnp.einsum(
        "htn,hnp->htp", out_heads, entering, precision=highest
    )
    outputs = state_out + skip_gain[:, None, None] * inputs_wide
    inverse = lax.rsqrt(jnp.mean(outputs * outputs, axis=2, keepdims=True) + epsilon)
    normed = outputs * inverse
    residual = normed - target
    grad_out = (residual - normed * jnp.mean(residual * normed, axis=2, keepdims=True)) * inverse
    local_dx = jnp.einsum("hts,htp->hsp", mixing, grad_out, precision=highest)
    cross = jnp.einsum("htp,hsp->hts", grad_out, inputs_wide, precision=highest)
    paired = decayed * cross
    local_din = jnp.einsum("hts,htn->hsn", paired, out_heads, precision=highest)
    grad_output_maps = jnp.einsum("hts,hsn->htn", paired, in_heads, precision=highest)
    grad_output_maps = grad_output_maps + from_start[..., None] * jnp.einsum(
        "hnp,htp->htn", entering, grad_out, precision=highest
    )
    forward_term = jnp.sum(grad_out * state_out, axis=2)
    flow = jnp.einsum(
        "htn,htp->hnp", out_heads * from_start[..., None], grad_out, precision=highest
    )
    closing = jnp.sum(forward_term - jnp.sum(inputs_wide * local_dx, axis=2), axis=1)
    identity = (
        jnp.ones_like(decays),
        jnp.zeros_like(flow),
        jnp.zeros_like(end_state),
        jnp.zeros_like(closing),
    )
    unused_decay, incoming, unused_state, later_sum = prefix(
        (decays, flow, end_state, closing), "seq", backward_chain, identity
    )
    state_dx = local_dx + jnp.einsum("hsn,hnp->hsp", weighted_in, incoming, precision=highest)
    terms = forward_term - jnp.sum(inputs_wide * state_dx, axis=2)
    grad_log_decay = later_sum[:, None] + lax.cumsum(terms, axis=1, reverse=True)
    grad_input_maps = (
        local_din
        + jnp.einsum("hnp,hsp->hsn", incoming, inputs_wide, precision=highest) * to_end[..., None]
    )
    grad_maps = jnp.concatenate([grad_input_maps, grad_output_maps], axis=2)
    grad_maps = grad_maps.reshape(local_groups, per_group, tok_dev, 2 * state_size).sum(axis=1)
    grad_x = state_dx + skip_gain[:, None, None] * grad_out
    return (grad_x.astype(jnp.bfloat16), grad_maps.astype(jnp.bfloat16), grad_log_decay)


def solution(mesh):
    in_specs = (
        P(("head", "sub"), ("groups", "seq"), None),
        P(("head", "sub"), ("groups", "seq"), None),
        P(("head", "sub"), ("groups", "seq"), None),
        P(("head", "sub"), ("groups", "seq"), None),
        P(("head", "sub"), ("groups", "seq")),
        P(("head", "sub")),
        P(("groups", "head", "sub"), None, None),
    )
    out_specs = (
        P(("head", "sub"), ("groups", "seq"), None),
        P(("head", "sub"), ("groups", "seq"), None),
        P(("head", "sub"), ("groups", "seq")),
    )
    return jax.shard_map(body, mesh=mesh, in_specs=in_specs, out_specs=out_specs, check_vma=False)
```

profile of v0, /device:TPU:0, one launch (start us, length us, event | category | flops | bytes accessed | tf_op | source)
XLA Modules:
  0.0 146.4 jit_solution(11512429082375482874)
XLA Ops:
  10.9 6.3 %all-to-all-start = ((bf16[2,8,128,128]{3,2,0,1:T(8,128)(2,1)}), bf16[2,8,128,128]{3,2,0,1:T(8,128)(2,1)S(1)}, u32[]{:S(2)}, u32[]{:S(2)}) async-start(bf16[2,8,128,128]{3,2,0,1:T(8,128)(2,1)} %copy.89), calls=%async_computation | async-start | bytes 1048576 | tf_op jit(solution)/shard_map/all_to_all | solution.py:124
  19.9 18.1 %all-reduce = bf16[64]{0:T(256)(128)(2,1)S(1)} all-reduce(bf16[64]{0:T(256)(128)(2,1)S(1)} %dynamic-update-slice), channel_id=2, replica_groups=mesh['groups'=2,'seq'=4,'head'=2,'sub'=2] {'seq'}, use_global_device_ids=true, to_apply=%add | all-reduce | flops 64 | bytes 256
  39.3 23.4 %all_gather.30 = bf16[2,512,256]{2,1,0:T(8,128)(2,1)} all-gather(bf16[2,128,256]{2,1,0:T(8,128)(2,1)S(1)} %copy-done.17), channel_id=1, replica_groups=mesh['groups'=2,'seq'=4,'head'=2,'sub'=2] {'seq'}, dimensions={1}, use_global_device_ids=true | all-gather | bytes 655360 | tf_op jit(solution)/shard_map/all_gather | solution.py:62
  62.8 2.2 %fusion.49 = f32[16,128,128]{1,2,0:T(8,128)} fusion(f32[16,128,128]{2,1,0:T(8,128)S(1)} %bitcast_multiply_fusion.1, bf16[16,128,128]{2,1,0:T(8,128)(2,1)S(1)} %copy-done), kind=kOutput, calls=%fused_computation.102 | convolution fusion | flops 402653184 | bytes 2621440 | tf_op jit(solution)/shard_map/hts,hsp->htp/dot_general | solution.py:158
  65.0 13.6 %while.49 = (s32[]{:T(128)}, f32[2,1024]{1,0:T(2,128)S(1)}, f32[2,1024]{1,0:T(2,128)S(1)}, f32[2,1024,128]{2,1,0:T(8,128)S(1)}, bf16[2,512,256]{2,1,0:T(8,128)(2...) while((s32[]{:T(128)}, f32[2,1024]{1,0:T(2,128)S(1)}, ...), condition=%wide.region_7.8_spmd.clone, body=%wide.region_4.7_spmd.clone.sunk | while | flops 137505920 | bytes 6563051 | solution.py:92
  66.8 1.6 %convolution_add_fusion.5 = f32[2,1024,128]{2,1,0:T(8,128)S(1)} fusion(f32[2,1024,128]{2,1,0:T(8,128)S(1)} %get-tuple-element.598, f32[2,1024,128]{1,2,0:T(8,128)S(1)} %get-tuple-element.553, f32[2,1024]{1,0:T(2,128)S(1)} %get-tuple-element.555, f32[2,1024]{1,0:T(2,128)S(1)} %fusion.87, pred[]{:T(512)S(6)} %compare.10, ...), kind=kOutput, calls=%fused_computation.14.clone.1 | convolution fusion | flops 68681728 | bytes 3358729 | tf_op jit(solution)/shard_map/while/body/eval_jaxpr/grk,gkd->grd/dot_general | solution.py:84
  70.2 1.6 %convolution_add_fusion.5 = f32[2,1024,128]{2,1,0:T(8,128)S(1)} fusion(f32[2,1024,128]{2,1,0:T(8,128)S(1)} %get-tuple-element.598, f32[2,1024,128]{1,2,0:T(8,128)S(1)} %get-tuple-element.553, f32[2,1024]{1,0:T(2,128)S(1)} %get-tuple-element.555, f32[2,1024]{1,0:T(2,128)S(1)} %fusion.87, pred[]{:T(512)S(6)} %compare.10, ...), kind=kOutput, calls=%fused_computation.14.clone.1 | convolution fusion | flops 68681728 | bytes 3358729 | tf_op jit(solution)/shard_map/while/body/eval_jaxpr/grk,gkd->grd/dot_general | solution.py:84
  73.6 1.6 %convolution_add_fusion.5 = f32[2,1024,128]{2,1,0:T(8,128)S(1)} fusion(f32[2,1024,128]{2,1,0:T(8,128)S(1)} %get-tuple-element.598, f32[2,1024,128]{1,2,0:T(8,128)S(1)} %get-tuple-element.553, f32[2,1024]{1,0:T(2,128)S(1)} %get-tuple-element.555, f32[2,1024]{1,0:T(2,128)S(1)} %fusion.87, pred[]{:T(512)S(6)} %compare.10, ...), kind=kOutput, calls=%fused_computation.14.clone.1 | convolution fusion | flops 68681728 | bytes 3358729 | tf_op jit(solution)/shard_map/while/body/eval_jaxpr/grk,gkd->grd/dot_general | solution.py:84
  77.0 1.6 %convolution_add_fusion.5 = f32[2,1024,128]{2,1,0:T(8,128)S(1)} fusion(f32[2,1024,128]{2,1,0:T(8,128)S(1)} %get-tuple-element.598, f32[2,1024,128]{1,2,0:T(8,128)S(1)} %get-tuple-element.553, f32[2,1024]{1,0:T(2,128)S(1)} %get-tuple-element.555, f32[2,1024]{1,0:T(2,128)S(1)} %fusion.87, pred[]{:T(512)S(6)} %compare.10, ...), kind=kOutput, calls=%fused_computation.14.clone.1 | convolution fusion | flops 68681728 | bytes 3358729 | tf_op jit(solution)/shard_map/while/body/eval_jaxpr/grk,gkd->grd/dot_general | solution.py:84
  80.0 3.5 %all-to-all-start.1 = ((bf16[2,8,128,128]{2,3,0,1:T(8,128)(2,1)}), bf16[2,8,128,128]{2,3,0,1:T(8,128)(2,1)S(1)}, u32[]{:S(2)}, u32[]{:S(2)}) async-start(bf16[2,8,128,128]{2,3,0,1:T(8,128)(2,1)} %copy.91), calls=%async_computation.1 | async-start | bytes 1048576 | tf_op jit(solution)/shard_map/all_to_all | solution.py:132
  85.1 3.3 %multiply_reduce_fusion.3 = (f32[16,128]{1,0:T(8,128)S(1)}, f32[16,128,128]{1,2,0:T(8,128)S(1)}) fusion(bf16[16,128,128]{1,2,0:T(8,128)(2,1)S(1)} %copy.88, f32[16]{0:T(128)S(1)} %copy-done.18, f32[16,128,128]{1,2,0:T(8,128)} %fusion.49, f32[16,128,64]{1,2,0:T(8,128)S(1)} %bitcast.93, f32[16,64,128]{2,1,0:T(8,128)S(1)} %get-tuple-element.293, ...), kind=kOutput, calls=%fused_computation.67 | convolution fusion | flops 203421696 | bytes 4210816 | tf_op jit(solution)/shard_map/htn,hnp->htp/dot_general | solution.py:168
  88.4 5.4 %all-to-all-done.1 = bf16[2,8,128,128]{2,3,0,1:T(8,128)(2,1)S(1)} async-done(((bf16[2,8,128,128]{2,3,0,1:T(8,128)(2,1)}), bf16[2,8,128,128]{2,3,0,1:T(8,128)(2,1)S(1)}, u32[]{:S(2)}, u32[]{:S(2)}) %all-to-all-start.1) | async-done | bytes 524320 | tf_op jit(solution)/shard_map/all_to_all | solution.py:132
  95.5 2.8 %convolution_convert_fusion = bf16[16,64,128]{2,1,0:T(8,128)(2,1)} fusion(f32[16,128,128]{1,2,0:T(8,128)S(1)} %get-tuple-element.394, f32[16,128,64]{1,2,0:T(8,128)S(1)} %bitcast.94, f32[16,128]{1,0:T(8,128)S(1)} %get-tuple-element.404), kind=kOutput, calls=%fused_computation.51 | convolution fusion | flops 201588736 | bytes 1843200 | tf_op jit(solution)/shard_map/htn,htp->hnp/dot_general | solution.py:185
  98.3 2.2 %fusion.28 = (f32[16,128]{1,0:T(8,128)S(1)}, f32[16,128,128]{1,2,0:T(8,128)}) fusion(bf16[16,128,128]{1,2,0:T(8,128)(2,1)S(1)} %copy.88, f32[16,128,128]{2,1,0:T(8,128)S(1)} %copy-done.3, f32[16,128,128]{1,2,0:T(8,128)S(1)} %get-tuple-element.394), kind=kOutput, calls=%fused_computation.54 | convolution fusion | flops 403437568 | bytes 3678208 | tf_op jit(solution)/shard_map/hts,htp->hsp/dot_general | solution.py:176
  100.9 10.3 %all-reduce.1 = bf16[64]{0:T(256)(128)(2,1)S(1)} all-reduce(bf16[64]{0:T(256)(128)(2,1)S(1)} %dynamic-update-slice.1), channel_id=5, replica_groups=mesh['groups'=2,'seq'=4,'head'=2,'sub'=2] {'seq'}, use_global_device_ids=true, to_apply=%add.1 | all-reduce | flops 64 | bytes 256
  111.2 2.2 %convolution_multiply_fusion.3 = f32[16,128,64]{1,2,0:T(8,128)S(1)} fusion(f32[16,128,128]{1,2,0:T(8,128)S(1)} %get-tuple-element.394, f32[16,128]{1,0:T(8,128)S(1)} %get-tuple-element.404, f32[16,64,128]{2,1,0:T(8,128)S(1)} %get-tuple-element.293, f32[16,64,128]{2,1,0:T(8,128)} %param.19, f32[16]{0:T(128)S(1)} %get-tuple-element.294), kind=kOutput, calls=%fused_computation.46 | convolution fusion | flops 201719808 | bytes 2629696 | tf_op jit(solution)/shard_map/hnp,htp->htn/dot_general | solution.py:181
  115.7 2.9 %convolution_add_fusion.2 = f32[16,128,64]{1,2,0:T(8,128)} fusion(f32[16,128,64]{1,2,0:T(8,128)S(1)} %convolution_multiply_fusion.3, f32[16,128,128]{2,1,0:T(8,128)S(1)} %convolution_multiply_fusion.1, f32[16,128,64]{1,2,0:T(8,128)S(1)} %bitcast.97), kind=kOutput, calls=%fused_computation.47 | convolution fusion | flops 201457664 | bytes 2621440 | tf_op jit(solution)/shard_map/hts,hsn->htn/dot_general | solution.py:180
  118.6 7.5 %all-gather.9.cloned.1.call-done = bf16[64,64,128]{2,1,0:T(8,128)(2,1)} async-done(((bf16[16,64,128]{2,1,0:T(8,128)(2,1)}), bf16[64,64,128]{2,1,0:T(8,128)(2,1)}) %all-gather.9.cloned.1.call-update) | async-done | bytes 1048592 | tf_op jit(solution)/shard_map/all_gather | solution.py:36
  126.1 4.4 %while.48 = (s32[]{:T(128)}, f32[16,64,128]{2,1,0:T(8,128)S(1)}, f32[16]{0:T(128)S(1)}, s32[]{:T(128)}, bf16[4,16]{1,0:T(4,128)(2,1)S(1)}, /*index=5*/bf16[4,16,...) while((s32[]{:T(128)}, f32[16,64,128]{2,1,0:T(8,128)S(1)}, ...), condition=%wide.region_15.16_spmd, body=%wide.region_13.15_spmd.sunk | while | flops 786486 | bytes 1573487 | solution.py:53
  126.2 1.3 fusion.81
  127.5 1.3 fusion.81
  128.9 1.3 fusion.81
  131.7 2.8 %fusion.29 = (f32[16,128]{1,0:T(8,128)S(1)}, bf16[16,128,128]{1,2,0:T(8,128)(2,1)}) fusion(bf16[16,128,128]{1,2,0:T(8,128)(2,1)S(1)} %copy.88, f32[16,128,128]{1,2,0:T(8,128)S(1)} %get-tuple-element.394, f32[16]{0:T(128)S(1)} %copy-done.18, f32[16,128,128]{1,2,0:T(8,128)S(1)} %copy-done.11, f32[16,64,128]{2,1,0:T(8,128)S(1)} %get-tuple-element.297, ...), kind=kOutput, calls=%fused_computation.55 | convolution fusion | flops 203290624 | bytes 4210752 | tf_op jit(solution)/shard_map/hsn,hnp->hsp/dot_general | solution.py:198
  137.6 1.2 reduce_window_sum.22
  (135 shorter events, 26.1 us)
Async XLA Ops:
  7.2 1.4 copy-start.15
  7.2 1.7 %copy-start = (bf16[16,128,128]{2,1,0:T(8,128)(2,1)S(1)}, bf16[16,128,128]{2,1,0:T(8,128)(2,1)}, u32[]{:S(2)}) copy-start(bf16[16,128,128]{2,1,0:T(8,128)(2,1)} %param.15) | copy-start | bytes 1572868
  7.2 76.4 %all-gather.7.cloned.1.call-start = ((), (), s32[]{:S(2)}) async-start(), calls=%async_computation.2 | async-start | bytes 1310720 | tf_op jit(solution)/shard_map/all_gather | solution.py:14
  8.8 1.3 copy-start.9
  8.8 1.3 copy-start.16
  10.9 54.0 %all-to-all-start = ((bf16[2,8,128,128]{3,2,0,1:T(8,128)(2,1)}), bf16[2,8,128,128]{3,2,0,1:T(8,128)(2,1)S(1)}, u32[]{:S(2)}, u32[]{:S(2)}) async-start(bf16[2,8,128,128]{3,2,0,1:T(8,128)(2,1)} %copy.89), calls=%async_computation | async-start | bytes 1048576 | tf_op jit(solution)/shard_map/all_to_all | solution.py:124
  17.8 0.7 copy-start.19
  38.4 0.9 copy-start.17
  38.8 24.0 %copy-start.2 = (f32[16,128,128]{2,1,0:T(8,128)}, f32[16,128,128]{2,1,0:T(8,128)S(1)}, u32[]{:S(2)}) copy-start(f32[16,128,128]{2,1,0:T(8,128)S(1)} %bitcast_multiply_fusion.1) | copy-start | bytes 3145732
  80.0 13.7 %all-to-all-start.1 = ((bf16[2,8,128,128]{2,3,0,1:T(8,128)(2,1)}), bf16[2,8,128,128]{2,3,0,1:T(8,128)(2,1)S(1)}, u32[]{:S(2)}, u32[]{:S(2)}) async-start(bf16[2,8,128,128]{2,3,0,1:T(8,128)(2,1)} %copy.91), calls=%async_computation.1 | async-start | bytes 1048576 | tf_op jit(solution)/shard_map/all_to_all | solution.py:132
  83.5 42.5 %all-gather.9.cloned.1.call-start = ((), (), s32[]{:S(2)}) async-start(), calls=%async_computation.3 | async-start | bytes 1310720 | tf_op jit(solution)/shard_map/all_gather | solution.py:36
  83.8 1.2 copy-start.14
  83.9 4.4 %copy-start.6 = (f32[2,8,128,64]{2,3,1,0:T(8,128)}, f32[2,8,128,64]{2,3,1,0:T(8,128)S(1)}, u32[]{:S(2)}) copy-start(f32[2,8,128,64]{2,3,1,0:T(8,128)S(1)} %broadcast_in_dim.109) | copy-start | bytes 1572868
  83.9 1.2 copy-start.18
  94.4 1.0 copy-start.7
  95.5 2.9 %copy-start.3 = (f32[16,128,128]{2,1,0:T(8,128)S(1)}, f32[16,128,128]{2,1,0:T(8,128)}, u32[]{:S(2)}) copy-start(f32[16,128,128]{2,1,0:T(8,128)} %copy-done.2) | copy-start | bytes 3145732
  111.2 2.2 %copy-start.1 = (bf16[16,128,128]{2,1,0:T(8,128)(2,1)S(1)}, bf16[16,128,128]{2,1,0:T(8,128)(2,1)}, u32[]{:S(2)}) copy-start(bf16[16,128,128]{2,1,0:T(8,128)(2,1)} %param.15) | copy-start | bytes 1572868
  113.4 2.2 %copy-start.10 = (f32[2,8,128,64]{2,3,1,0:T(8,128)S(1)}, f32[2,8,128,64]{2,3,1,0:T(8,128)}, u32[]{:S(2)}) copy-start(f32[2,8,128,64]{2,3,1,0:T(8,128)} %copy-done.9) | copy-start | bytes 1572868
  114.7 1.0 copy-start.4
  130.5 1.2 copy-start.11
  131.7 2.8 %copy-start.5 = (f32[16,128,128]{2,1,0:T(8,128)S(1)}, f32[16,128,128]{2,1,0:T(8,128)}, u32[]{:S(2)}) copy-start(f32[16,128,128]{2,1,0:T(8,128)} %copy-done.4) | copy-start | bytes 3145732
  131.7 2.8 %copy-start.8 = (f32[2,8,128,64]{2,3,1,0:T(8,128)S(1)}, f32[2,8,128,64]{2,3,1,0:T(8,128)}, u32[]{:S(2)}) copy-start(f32[2,8,128,64]{2,3,1,0:T(8,128)} %copy-done.6) | copy-start | bytes 1572868
  134.5 1.1 copy-start.12
  135.6 1.0 copy-start.13
Sparse Core Ops, SparseCore 0:
  10.2 41.8 all-gather.6
  98.5 27.5 all-gather.8
where the time goes:
time: 147 us; the launch traced here: 146 us
  blocking collectives  51.8 us (35%)
  matrix products  34.5 us (23%)
  between operations  15.2 us (10%)
  waiting for transfers between devices  12.9 us (9%)
  other arithmetic  11.2 us (8%)
  local copies, waits for them, and re-layouts  10.1 us (7%)
  starting transfers between devices  9.87 us (7%)
    unnamed x2, blocking collectives  28.3 us
    all_gather x1, blocking collectives, attend(): shards = lax.all_gather(keys_values, 'seq', axis=1, tiled=True)  23.4 us
    unnamed x51, local copies, waits for them, and re-layouts  7.57 us
    all_gather x1, waiting for transfers between devices, prefix(): lax.all_gather(a.astype(kind), axis)  7.49 us
    dot_general x4, matrix products, one_block(): jnp.einsum('grk,gkd->grd', weights.astype(jnp.bfloat16), key_block[:, :,...  6.51 us
    all_to_all x1, starting transfers between devices, body(): lax.all_to_all(sectioned, 'seq', split_axis=1, concat_axis=1, tiled=True)  6.32 us
    all_to_all x1, waiting for transfers between devices, body(): lax.all_to_all(answers, 'seq', split_axis=1, concat_axis=1, tiled=True)  5.39 us
    dot_general x4, matrix products, one_block(): jnp.einsum('grd,gkd->grk', query_rows, key_block[:, :, :head_width], pref...  4.86 us
  transfers between devices with their start and end apart: 4, of which 2 were waited for; matrix products, arithmetic and copies ran while one was open for 22% of the time, Pallas kernels for 0%

commit v1 on v0

--- a/solution.py
+++ b/solution.py
@@ -59,7 +59,12 @@
     start_max = jnp.full((group_count, row_count), -1e30, jnp.float32)
     start_sum = jnp.zeros((group_count, row_count), jnp.float32)
     start_acc = jnp.zeros((group_count, row_count, head_width), jnp.float32)
-    shards = lax.all_gather(keys_values, "seq", axis=1, tiled=True)
+    ring = [keys_values]
+    for hop in range(3):
+        ring.append(lax.ppermute(ring[-1], "seq", [(dev, (dev + 1) % 4) for dev in range(4)]))
+    shards = jnp.roll(
+        jnp.concatenate(ring[::-1], axis=1), (lax.axis_index("seq") + 1) * ring[0].shape[1], axis=1
+    )
     block_rows = math.gcd(shards.shape[1], tok_dev)
 
     def one_block(number, running):

time: 147 us -> 142 us (0.966)
  blocking collectives: 51.8 us -> 28.7 us
  waiting for transfers between devices: 12.9 us -> 22.9 us
  local copies, waits for them, and re-layouts: 10.1 us -> 13.6 us
  starting transfers between devices: 9.87 us -> 13.2 us
    all_gather x1 -> x0, blocking collectives: 23.4 us -> none  [attend(): shards = lax.all_gather(keys_values, 'seq', axis=1, tiled=True)]
    ppermute x0 -> x3, waiting for transfers between devices: none -> 16.3 us  [attend(): lax.ppermute(ring[-1], 'seq', [(dev, (dev + 1) % 4) for dev in range(4)])]
    ppermute x0 -> x3, starting transfers between devices: none -> 5.66 us  [attend(): lax.ppermute(ring[-1], 'seq', [(dev, (dev + 1) % 4) for dev in range(4)])]
    all_to_all x1, waiting for transfers between devices: 5.39 us -> 0.01 us  [body(): lax.all_to_all(answers, 'seq', split_axis=1, concat_axis=1, tiled=True)]
    all_to_all x1, starting transfers between devices: 6.32 us -> 3.99 us  [body(): lax.all_to_all(sectioned, 'seq', split_axis=1, concat_axis=1, tiled=True)]
    unnamed x51 -> x50, local copies, waits for them, and re-layouts: 7.57 us -> 9.14 us
  transfers between devices with their start and end apart: 4 -> 7, of which waited for: 2 -> 3; matrix products, arithmetic and copies ran while one was open for 22% -> 24% of each run, Pallas kernels for 0% -> 0%
where the time goes in v1:
time: 142 us; the launch traced here: 140 us
  matrix products  35.8 us (25%)
  blocking collectives  28.7 us (20%)
  waiting for transfers between devices  22.9 us (16%)
  between operations  15.1 us (11%)
  local copies, waits for them, and re-layouts  13.6 us (10%)
  starting transfers between devices  13.2 us (9%)
  other arithmetic  10.5 us (7%)
    unnamed x2, blocking collectives  28.7 us
    ppermute x3, waiting for transfers between devices, attend(): lax.ppermute(ring[-1], 'seq', [(dev, (dev + 1) % 4) for dev in range(4)])  16.3 us
    unnamed x50, local copies, waits for them, and re-layouts  9.14 us
    dot_general x4, matrix products, one_block(): jnp.einsum('grk,gkd->grd', weights.astype(jnp.bfloat16), key_block[:, :,...  6.52 us
    all_gather x1, waiting for transfers between devices, prefix(): lax.all_gather(a.astype(kind), axis)  6.48 us
    ppermute x3, starting transfers between devices, attend(): lax.ppermute(ring[-1], 'seq', [(dev, (dev + 1) % 4) for dev in range(4)])  5.66 us
    dot_general x4, matrix products, one_block(): jnp.einsum('grd,gkd->grk', query_rows, key_block[:, :, :head_width], pref...  4.86 us
    all_to_all x1, starting transfers between devices, body(): lax.all_to_all(sectioned, 'seq', split_axis=1, concat_axis=1, tiled=True)  3.99 us
  transfers between devices with their start and end apart: 7, of which 3 were waited for; matrix products, arithmetic and copies ran while one was open for 24% of the time, Pallas kernels for 0%

profile of v1, /device:TPU:0, one launch (start us, length us, event | category | flops | bytes accessed | tf_op | source)
XLA Modules:
  0.0 140.5 jit_solution(10552049607273684000)
XLA Ops:
  7.2 3.1 %collective-permute-start = (bf16[2,128,256]{2,1,0:T(8,128)(2,1)}, bf16[2,128,256]{2,1,0:T(8,128)(2,1)S(1)}, u32[]{:S(2)}, u32[]{:S(2)}) collective-permute-start(bf16[2,128,256]{2,1,0:T(8,128)(2,1)} %param.14), channel_id=1, source_target_pairs={{0,4},{4,8},{8,12},{12,0},{1,5},{5,9},{9,13},{13,1},{2,6},{6,10},{... | collective-permute-start | bytes 393224 | tf_op jit(solution)/shard_map/ppermute | solution.py:64
  10.2 1.9 %copy.89 = bf16[2,8,128,128]{3,2,0,1:T(8,128)(2,1)} copy(bf16[2,8,128,128]{3,2,1,0:T(8,128)(2,1)} %bitcast.102) | data formatting | bytes 1048576 | tf_op jit(solution)/shard_map/reshape | solution.py:128
  12.2 4.0 %all-to-all-start = ((bf16[2,8,128,128]{3,2,0,1:T(8,128)(2,1)}), bf16[2,8,128,128]{3,2,0,1:T(8,128)(2,1)S(1)}, u32[]{:S(2)}, u32[]{:S(2)}) async-start(bf16[2,8,128,128]{3,2,0,1:T(8,128)(2,1)} %copy.89), calls=%async_computation | async-start | bytes 1048576 | tf_op jit(solution)/shard_map/all_to_all | solution.py:129
  16.9 2.1 %collective-permute-start.1 = (bf16[2,128,256]{2,1,0:T(8,128)(2,1)S(1)}, bf16[2,128,256]{2,1,0:T(8,128)(2,1)S(1)}, u32[]{:S(2)}, u32[]{:S(2)}) collective-permute-start(bf16[2,128,256]{2,1,0:T(8,128)(2,1)S(1)} %collective-permute-done), channel_id=1, source_target_pairs={{0,4},{4,8},{8,12},{12,0},{1,5},{5,9},{9,13},{13,1},{2,6},{6,10},{... | collective-permute-start | bytes 393224 | tf_op jit(solution)/shard_map/ppermute | solution.py:64
  19.0 12.3 %collective-permute-done.1 = bf16[2,128,256]{2,1,0:T(8,128)(2,1)S(1)} collective-permute-done((bf16[2,128,256]{2,1,0:T(8,128)(2,1)S(1)}, bf16[2,128,256]{2,1,0:T(8,128)(2,1)S(1)}, u32[]{:S(2)}, u32[]{:S(2)}) %collective-permute-start.1) | collective-permute-done | bytes 131104 | tf_op jit(solution)/shard_map/ppermute | solution.py:64
  34.0 4.0 %collective-permute-done.2 = bf16[2,128,256]{2,1,0:T(8,128)(2,1)S(1)} collective-permute-done((bf16[2,128,256]{2,1,0:T(8,128)(2,1)S(1)}, bf16[2,128,256]{2,1,0:T(8,128)(2,1)S(1)}, u32[]{:S(2)}, u32[]{:S(2)}) %collective-permute-start.2) | collective-permute-done | bytes 131104 | tf_op jit(solution)/shard_map/ppermute | solution.py:64
  40.0 13.6 %while.49 = (s32[]{:T(128)}, f32[2,1024]{1,0:T(2,128)S(1)}, f32[2,1024]{1,0:T(2,128)S(1)}, f32[2,1024,128]{2,1,0:T(8,128)S(1)}, bf16[2,512,256]{2,1,0:T(8,128)(2...) while((s32[]{:T(128)}, f32[2,1024]{1,0:T(2,128)S(1)}, ...), condition=%wide.region_7.8_spmd.clone, body=%wide.region_4.7_spmd.clone.sunk | while | flops 137505920 | bytes 6563051 | solution.py:97
  41.7 1.6 %convolution_add_fusion.5 = f32[2,1024,128]{2,1,0:T(8,128)S(1)} fusion(f32[2,1024,128]{2,1,0:T(8,128)S(1)} %get-tuple-element.598, f32[2,1024,128]{1,2,0:T(8,128)S(1)} %get-tuple-element.553, f32[2,1024]{1,0:T(2,128)S(1)} %get-tuple-element.555, f32[2,1024]{1,0:T(2,128)S(1)} %fusion.87, pred[]{:T(512)S(6)} %compare.11, ...), kind=kOutput, calls=%fused_computation.14.clone.1 | convolution fusion | flops 68681728 | bytes 3358729 | tf_op jit(solution)/shard_map/while/body/eval_jaxpr/grk,gkd->grd/dot_general | solution.py:89
  45.1 1.6 %convolution_add_fusion.5 = f32[2,1024,128]{2,1,0:T(8,128)S(1)} fusion(f32[2,1024,128]{2,1,0:T(8,128)S(1)} %get-tuple-element.598, f32[2,1024,128]{1,2,0:T(8,128)S(1)} %get-tuple-element.553, f32[2,1024]{1,0:T(2,128)S(1)} %get-tuple-element.555, f32[2,1024]{1,0:T(2,128)S(1)} %fusion.87, pred[]{:T(512)S(6)} %compare.11, ...), kind=kOutput, calls=%fused_computation.14.clone.1 | convolution fusion | flops 68681728 | bytes 3358729 | tf_op jit(solution)/shard_map/while/body/eval_jaxpr/grk,gkd->grd/dot_general | solution.py:89
  48.6 1.6 %convolution_add_fusion.5 = f32[2,1024,128]{2,1,0:T(8,128)S(1)} fusion(f32[2,1024,128]{2,1,0:T(8,128)S(1)} %get-tuple-element.598, f32[2,1024,128]{1,2,0:T(8,128)S(1)} %get-tuple-element.553, f32[2,1024]{1,0:T(2,128)S(1)} %get-tuple-element.555, f32[2,1024]{1,0:T(2,128)S(1)} %fusion.87, pred[]{:T(512)S(6)} %compare.11, ...), kind=kOutput, calls=%fused_computation.14.clone.1 | convolution fusion | flops 68681728 | bytes 3358729 | tf_op jit(solution)/shard_map/while/body/eval_jaxpr/grk,gkd->grd/dot_general | solution.py:89
  52.0 1.6 %convolution_add_fusion.5 = f32[2,1024,128]{2,1,0:T(8,128)S(1)} fusion(f32[2,1024,128]{2,1,0:T(8,128)S(1)} %get-tuple-element.598, f32[2,1024,128]{1,2,0:T(8,128)S(1)} %get-tuple-element.553, f32[2,1024]{1,0:T(2,128)S(1)} %get-tuple-element.555, f32[2,1024]{1,0:T(2,128)S(1)} %fusion.87, pred[]{:T(512)S(6)} %compare.11, ...), kind=kOutput, calls=%fused_computation.14.clone.1 | convolution fusion | flops 68681728 | bytes 3358729 | tf_op jit(solution)/shard_map/while/body/eval_jaxpr/grk,gkd->grd/dot_general | solution.py:89
  55.0 3.5 %all-to-all-start.1 = ((bf16[2,8,128,128]{2,3,0,1:T(8,128)(2,1)}), bf16[2,8,128,128]{2,3,0,1:T(8,128)(2,1)S(1)}, u32[]{:S(2)}, u32[]{:S(2)}) async-start(bf16[2,8,128,128]{2,3,0,1:T(8,128)(2,1)} %copy.91), calls=%async_computation.1 | async-start | bytes 1048576 | tf_op jit(solution)/shard_map/all_to_all | solution.py:137
  61.0 13.5 %all-reduce = bf16[64]{0:T(256)(128)(2,1)S(1)} all-reduce(bf16[64]{0:T(256)(128)(2,1)S(1)} %dynamic-update-slice), channel_id=2, replica_groups=mesh['groups'=2,'seq'=4,'head'=2,'sub'=2] {'seq'}, use_global_device_ids=true, to_apply=%add | all-reduce | flops 64 | bytes 256
  76.3 2.3 %fusion.49 = f32[16,128,128]{1,2,0:T(8,128)} fusion(f32[16,128,128]{2,1,0:T(8,128)S(1)} %bitcast_multiply_fusion.1, bf16[16,128,128]{2,1,0:T(8,128)(2,1)S(1)} %copy-done), kind=kOutput, calls=%fused_computation.111 | convolution fusion | flops 402653184 | bytes 2621440 | tf_op jit(solution)/shard_map/hts,hsp->htp/dot_general | solution.py:163
  80.0 3.3 %multiply_reduce_fusion.3 = (f32[16,128]{1,0:T(8,128)S(1)}, f32[16,128,128]{1,2,0:T(8,128)S(1)}) fusion(bf16[16,128,128]{1,2,0:T(8,128)(2,1)S(1)} %copy.88, f32[16]{0:T(128)S(1)} %copy-done.14, f32[16,128,128]{1,2,0:T(8,128)} %fusion.49, f32[16,128,64]{1,2,0:T(8,128)S(1)} %bitcast.93, f32[16,64,128]{2,1,0:T(8,128)S(1)} %get-tuple-element.293, ...), kind=kOutput, calls=%fused_computation.67 | convolution fusion | flops 203421696 | bytes 4210816 | tf_op jit(solution)/shard_map/htn,hnp->htp/dot_general | solution.py:173
  84.5 2.8 %convolution_convert_fusion = bf16[16,64,128]{2,1,0:T(8,128)(2,1)} fusion(f32[16,128,128]{1,2,0:T(8,128)S(1)} %get-tuple-element.394, f32[16,128,64]{1,2,0:T(8,128)S(1)} %bitcast.94, f32[16,128]{1,0:T(8,128)S(1)} %get-tuple-element.404), kind=kOutput, calls=%fused_computation.51 | convolution fusion | flops 201588736 | bytes 1843200 | tf_op jit(solution)/shard_map/htn,htp->hnp/dot_general | solution.py:190
  87.3 3.3 %fusion.28 = (f32[16,128]{1,0:T(8,128)S(1)}, f32[16,128,128]{1,2,0:T(8,128)}) fusion(bf16[16,128,128]{1,2,0:T(8,128)(2,1)S(1)} %copy.88, f32[16,128,128]{2,1,0:T(8,128)} %copy-done.1, f32[16,128,128]{1,2,0:T(8,128)S(1)} %get-tuple-element.394), kind=kOutput, calls=%fused_computation.54 | convolution fusion | flops 403437568 | bytes 3678208 | tf_op jit(solution)/shard_map/hts,htp->hsp/dot_general | solution.py:181
  91.0 15.1 %all-reduce.1 = bf16[64]{0:T(256)(128)(2,1)S(1)} all-reduce(bf16[64]{0:T(256)(128)(2,1)S(1)} %dynamic-update-slice.1), channel_id=5, replica_groups=mesh['groups'=2,'seq'=4,'head'=2,'sub'=2] {'seq'}, use_global_device_ids=true, to_apply=%add.1 | all-reduce | flops 64 | bytes 256
  106.3 2.1 %convolution_multiply_fusion.3 = f32[16,128,64]{1,2,0:T(8,128)S(1)} fusion(f32[16,128,128]{1,2,0:T(8,128)S(1)} %get-tuple-element.394, f32[16,128]{1,0:T(8,128)S(1)} %get-tuple-element.404, f32[16,64,128]{2,1,0:T(8,128)S(1)} %get-tuple-element.293, f32[16,64,128]{2,1,0:T(8,128)} %param.19, f32[16]{0:T(128)S(1)} %get-tuple-element.294), kind=kOutput, calls=%fused_computation.46 | convolution fusion | flops 201719808 | bytes 2629696 | tf_op jit(solution)/shard_map/hnp,htp->htn/dot_general | solution.py:186
  110.6 2.9 %convolution_add_fusion.2 = f32[16,128,64]{1,2,0:T(8,128)} fusion(f32[16,128,64]{1,2,0:T(8,128)S(1)} %convolution_multiply_fusion.3, f32[16,128,128]{2,1,0:T(8,128)S(1)} %convolution_multiply_fusion.1, f32[16,128,64]{1,2,0:T(8,128)S(1)} %bitcast.97), kind=kOutput, calls=%fused_computation.47 | convolution fusion | flops 201457664 | bytes 2621440 | tf_op jit(solution)/shard_map/hts,hsn->htn/dot_general | solution.py:185
  113.5 6.5 %all-gather.9.cloned.1.call-done = bf16[64,64,128]{2,1,0:T(8,128)(2,1)} async-done(((bf16[16,64,128]{2,1,0:T(8,128)(2,1)}), bf16[64,64,128]{2,1,0:T(8,128)(2,1)}) %all-gather.9.cloned.1.call-update) | async-done | bytes 1048592 | tf_op jit(solution)/shard_map/all_gather | solution.py:36
  120.1 4.4 %while.48 = (s32[]{:T(128)}, f32[16,64,128]{2,1,0:T(8,128)S(1)}, f32[16]{0:T(128)S(1)}, s32[]{:T(128)}, bf16[4,16]{1,0:T(4,128)(2,1)S(1)}, /*index=5*/bf16[4,16,...) while((s32[]{:T(128)}, f32[16,64,128]{2,1,0:T(8,128)S(1)}, ...), condition=%wide.region_15.16_spmd, body=%wide.region_13.15_spmd.sunk | while | flops 786486 | bytes 1573487 | solution.py:53
  121.5 1.3 fusion.81
  125.8 2.8 %fusion.29 = (f32[16,128]{1,0:T(8,128)S(1)}, bf16[16,128,128]{1,2,0:T(8,128)(2,1)}) fusion(bf16[16,128,128]{1,2,0:T(8,128)(2,1)S(1)} %copy.88, f32[16,128,128]{1,2,0:T(8,128)S(1)} %get-tuple-element.394, f32[16]{0:T(128)S(1)} %copy-done.14, f32[16,128,128]{1,2,0:T(8,128)S(1)} %copy-done.7, f32[16,64,128]{2,1,0:T(8,128)S(1)} %get-tuple-element.297, ...), kind=kOutput, calls=%fused_computation.55 | convolution fusion | flops 203290624 | bytes 4210752 | tf_op jit(solution)/shard_map/hsn,hnp->hsp/dot_general | solution.py:203
  (141 shorter events, 31.4 us)
Async XLA Ops:
  7.2 9.7 %collective-permute-start = (bf16[2,128,256]{2,1,0:T(8,128)(2,1)}, bf16[2,128,256]{2,1,0:T(8,128)(2,1)S(1)}, u32[]{:S(2)}, u32[]{:S(2)}) collective-permute-start(bf16[2,128,256]{2,1,0:T(8,128)(2,1)} %param.14), channel_id=1, source_target_pairs={{0,4},{4,8},{8,12},{12,0},{1,5},{5,9},{9,13},{13,1},{2,6},{6,10},{... | collective-permute-start | bytes 393224 | tf_op jit(solution)/shard_map/ppermute | solution.py:64
  12.1 4.0 %copy-start.11 = (bf16[2,128,128]{2,1,0:T(8,128)(2,1)S(1)}, bf16[2,128,128]{2,1,0:T(8,128)(2,1)}, u32[]{:S(2)}) copy-start(bf16[2,128,128]{2,1,0:T(8,128)(2,1)} %param.16) | copy-start | bytes 196612
  12.2 4.1 %copy-start.13 = (f32[16,128]{1,0:T(8,128)S(1)}, f32[16,128]{1,0:T(8,128)}, u32[]{:S(2)}) copy-start(f32[16,128]{1,0:T(8,128)} %param.17) | copy-start | bytes 24580
  12.2 27.8 %all-to-all-start = ((bf16[2,8,128,128]{3,2,0,1:T(8,128)(2,1)}), bf16[2,8,128,128]{3,2,0,1:T(8,128)(2,1)S(1)}, u32[]{:S(2)}, u32[]{:S(2)}) async-start(bf16[2,8,128,128]{3,2,0,1:T(8,128)(2,1)} %copy.89), calls=%async_computation | async-start | bytes 1048576 | tf_op jit(solution)/shard_map/all_to_all | solution.py:129
  16.1 16.5 %copy-start = (bf16[16,128,128]{2,1,0:T(8,128)(2,1)S(1)}, bf16[16,128,128]{2,1,0:T(8,128)(2,1)}, u32[]{:S(2)}) copy-start(bf16[16,128,128]{2,1,0:T(8,128)(2,1)} %param.15) | copy-start | bytes 1572868
  16.1 62.6 %all-gather.7.cloned.1.call-start = ((), (), s32[]{:S(2)}) async-start(), calls=%async_computation.2 | async-start | bytes 1310720 | tf_op jit(solution)/shard_map/all_gather | solution.py:14
  16.9 14.4 %collective-permute-start.1 = (bf16[2,128,256]{2,1,0:T(8,128)(2,1)S(1)}, bf16[2,128,256]{2,1,0:T(8,128)(2,1)S(1)}, u32[]{:S(2)}, u32[]{:S(2)}) collective-permute-start(bf16[2,128,256]{2,1,0:T(8,128)(2,1)S(1)} %collective-permute-done), channel_id=1, source_target_pairs={{0,4},{4,8},{8,12},{12,0},{1,5},{5,9},{9,13},{13,1},{2,6},{6,10},{... | collective-permute-start | bytes 393224 | tf_op jit(solution)/shard_map/ppermute | solution.py:64
  31.3 6.8 %collective-permute-start.2 = (bf16[2,128,256]{2,1,0:T(8,128)(2,1)S(1)}, bf16[2,128,256]{2,1,0:T(8,128)(2,1)S(1)}, u32[]{:S(2)}, u32[]{:S(2)}) collective-permute-start(bf16[2,128,256]{2,1,0:T(8,128)(2,1)S(1)} %collective-permute-done.1), channel_id=1, source_target_pairs={{0,4},{4,8},{8,12},{12,0},{1,5},{5,9},{9,13},{13,1},{2,6},{6,10},{... | collective-permute-start | bytes 393224 | tf_op jit(solution)/shard_map/ppermute | solution.py:64
  31.9 0.8 copy-start.4
  38.1 0.9 copy-start.12
  55.0 23.6 %all-to-all-start.1 = ((bf16[2,8,128,128]{2,3,0,1:T(8,128)(2,1)}), bf16[2,8,128,128]{2,3,0,1:T(8,128)(2,1)S(1)}, u32[]{:S(2)}, u32[]{:S(2)}) async-start(bf16[2,8,128,128]{2,3,0,1:T(8,128)(2,1)} %copy.91), calls=%async_computation.1 | async-start | bytes 1048576 | tf_op jit(solution)/shard_map/all_to_all | solution.py:137
  58.5 61.6 %all-gather.9.cloned.1.call-start = ((), (), s32[]{:S(2)}) async-start(), calls=%async_computation.3 | async-start | bytes 1310720 | tf_op jit(solution)/shard_map/all_gather | solution.py:36
  58.8 0.7 copy-start.15
  75.3 1.0 copy-start.1
  79.0 1.0 copy-start.10
  79.1 1.0 copy-start.14
  108.4 2.2 %copy-start.5 = (f32[2,8,128,64]{2,3,1,0:T(8,128)S(1)}, f32[2,8,128,64]{2,3,1,0:T(8,128)}, u32[]{:S(2)}) copy-start(f32[2,8,128,64]{2,3,1,0:T(8,128)} %copy-done.4) | copy-start | bytes 1572868
  109.6 1.0 copy-start.2
  124.5 1.2 copy-start.7
  124.5 1.3 copy-start.6
  125.8 2.8 %copy-start.3 = (f32[16,128,128]{2,1,0:T(8,128)S(1)}, f32[16,128,128]{2,1,0:T(8,128)}, u32[]{:S(2)}) copy-start(f32[16,128,128]{2,1,0:T(8,128)} %copy-done.2) | copy-start | bytes 3145732
  128.6 1.0 copy-start.8
  129.7 1.0 copy-start.9
Sparse Core Ops, SparseCore 0:
  34.1 33.4 all-gather.6
  87.4 32.5 all-gather.8
